TPU v7x, 256 devices: a whole 4x4x8 slice. The times are simulated.
256 devices in a mesh: tm: 32 (over x_lo, z, core), cell: 8 (over y, x_hi).
Axes of the slice: x: 4 (x_hi: 2, x_lo: 2; x = x_hi * 2 + x_lo), y: 4, z: 8, core: 2. Of those that a mesh axis runs over, the one named last changes fastest.
Arguments:
- velocity: bfloat16 [4096, 512, 96], P('cell', 'tm'), may hold values from -6 to 6
- cell_coords: int32 [4096, 3], P('cell'), may hold values from 0 to 15, as said below
- q_coords: int32 [512, 3], replicated, may hold values from 0 to 15
- eigvecs: float32 [512, 2, 96, 96], P(('tm', 'cell')), may hold values from -0.4375 to 0.4375
Outputs:
- power: float32 [512, 96, 512], P(('tm', 'cell'))
Inputs may be any that keep to these rules, and one draw needn't show every extreme that they name: `cell_coords`: every row names a distinct lattice position, each coordinate in 0 to 15.
All inputs are finite; a program needn't handle non-finite values.
Results may differ from a plain program's by a relative error of at most 0.015.
Values may be sent and summed in bfloat16 or wider, within the bound.
No kernel may reach another device: no remote copies, remote signals or barrier semaphores. Data moves between devices by JAX's collectives and lax.ppermute only.
A program may use at most 64 MiB of HBM per device.

v0:
```python
import math
import jax
import jax.numpy as jnp
from jax import lax
from jax.sharding import PartitionSpec as P

L = 16


def phase_rows(q_coords, cell_coords):
    products = (
        q_coords[:, None, 0] * cell_coords[None, :, 0]
        + q_coords[:, None, 1] * cell_coords[None, :, 1]
        + q_coords[:, None, 2] * cell_coords[None, :, 2]
    ) % L
    angles = products.astype(jnp.float32) * (2.0 * math.pi / L)
    return jnp.stack([jnp.cos(angles), -jnp.sin(angles)], axis=1).astype(jnp.bfloat16)


def twiddles(frames):
    steps = jnp.arange(frames, dtype=jnp.int32)
    products = steps[:, None] * steps[None, :] % frames
    angles = products.astype(jnp.float32) * (2.0 * math.pi / frames)
    return (jnp.cos(angles), jnp.sin(angles))


def fourier(real_in, imag_in, cosines, sines, form):
    largest_value = lax.Precision.HIGHEST
    real_out = jnp.einsum(form, real_in, cosines, precision=largest_value) + jnp.einsum(
        form, imag_in, sines, precision=largest_value
    )
    imag_out = jnp.einsum(form, imag_in, cosines, precision=largest_value) - jnp.einsum(
        form, real_in, sines, precision=largest_value
    )
    return (real_out, imag_out)


def contract_modes(real_in, imag_in, eigvecs, form):
    largest_value = lax.Precision.HIGHEST
    eigenvector_real = eigvecs[:, 0]
    eigenvector_imaginary = eigvecs[:, 1]
    real_out = jnp.einsum(form, real_in, eigenvector_real, precision=largest_value) + jnp.einsum(
        form, imag_in, eigenvector_imaginary, precision=largest_value
    )
    imag_out = jnp.einsum(form, imag_in, eigenvector_real, precision=largest_value) - jnp.einsum(
        form, real_in, eigenvector_imaginary, precision=largest_value
    )
    return (real_out, imag_out)


def local(velocity, cell_coords, q_coords, eigvecs):
    n_tm = lax.axis_size("tm")
    n_cell = lax.axis_size("cell")
    cell_dev, frames_dev, branches = velocity.shape
    q_total = q_coords.shape[0]
    q_local = q_total // (n_tm * n_cell)
    owned_count = n_tm * q_local
    frames = frames_dev * n_tm
    cosines, sines = twiddles(frames)
    ordered_coords = (
        q_coords.reshape(n_tm, n_cell, q_local, 3).transpose(1, 0, 2, 3).reshape(q_total, 3)
    )
    phase_table = phase_rows(ordered_coords, cell_coords)
    velocity_rows = velocity.reshape(cell_dev, frames_dev * branches)
    partial_term = jnp.dot(
        phase_table.reshape(2 * q_total, cell_dev),
        velocity_rows,
        preferred_element_type=jnp.float32,
    )
    summed = (
        lax.psum(partial_term.astype(jnp.bfloat16), "cell")
        .astype(jnp.float32)
        .reshape(q_total, 2, frames_dev * branches)
    )
    owned_rows = lax.dynamic_slice_in_dim(
        summed, lax.axis_index("cell") * owned_count, owned_count, 0
    )
    owned_rows = owned_rows * (1.0 / math.sqrt(cell_dev * n_cell))
    blocks = owned_rows.reshape(n_tm, q_local, 2, frames_dev, branches)
    collected_rows = lax.all_to_all(
        blocks.astype(jnp.bfloat16), "tm", split_axis=0, concat_axis=3, tiled=True
    ).astype(blocks.dtype)[0]
    amplitude_real, amplitude_imaginary = contract_modes(
        collected_rows[:, 0], collected_rows[:, 1], eigvecs, "xcg,xga->xca"
    )
    out_real, out_imag = fourier(amplitude_real, amplitude_imaginary, cosines, sines, "qts,tw->qsw")
    return (out_real * out_real + out_imag * out_imag) / frames


def solution(mesh):
    in_specs = (P("cell", "tm", None), P("cell", None), P(), P(("tm", "cell"), None, None, None))
    out_specs = P(("tm", "cell"), None, None)
    return jax.shard_map(local, mesh=mesh, in_specs=in_specs, out_specs=out_specs, check_vma=False)
```

profile of v0, /device:TPU:1, one launch (start us, length us, event | category | flops | bytes accessed | tf_op | source)
XLA Modules:
  0.0 242.4 jit_solution(15547292508273227496)
XLA Ops:
  6.5 1.1 reshape.405
  7.7 0.1 copy.36
  7.8 0.3 reshape.406
  8.0 0.8 fusion.52
  8.9 5.0 %cosine_convert_fusion = (bf16[512,1,512]{2,0,1:T(8,128)(2,1)S(1)}, bf16[512,1,512]{2,0,1:T(8,128)(2,1)S(1)}) fusion(s32[512]{0:T(512)S(1)} %bitcast.73, s32[512]{0:T(512)S(1)} %bitcast.70, s32[512]{0:T(512)S(1)} %bitcast.74, s32[512]{0:T(512)S(1)} %bitcast.71, s32[512]{0:T(512)S(1)} %bitcast.72, s32[512]{0:T(512)S(1)} %bitcast.69), kind=kLoop, calls=%fused_computation.31 | loop fusion | flops 5505024 | bytes 1060864 | tf_op jit(solution)/shard_map/convert.1
  13.8 0.1 pad_maximum_fusion
  14.0 1.1 copy.37
  15.0 1.2 convert_element_type.46
  16.3 4.7 %convolution_convert_fusion = bf16[1024,1536]{1,0:T(8,128)(2,1)} fusion(bf16[1024,512]{1,0:T(8,128)(2,1)} %convert_element_type.46, bf16[512,1536]{0,1:T(8,128)(2,1)S(1)} %bitcast.62), kind=kOutput, calls=%fused_computation | convolution fusion | flops 1612185600 | bytes 5767168 | tf_op jit(solution)/shard_map/dot_general | solution.py:65
  21.0 7.2 %reshape.408 = bf16[512,2,1536]{2,1,0:T(2,128)(2,1)} reshape(bf16[1024,1536]{1,0:T(8,128)(2,1)} %convolution_convert_fusion) | data formatting | bytes 6291456 | tf_op jit(solution)/shard_map/reshape | solution.py:73
  28.2 4.0 %copy.38 = bf16[512,2,1536]{2,0,1:T(8,128)(2,1)} copy(bf16[512,2,1536]{2,1,0:T(2,128)(2,1)} %reshape.408) | data formatting | bytes 6291456 | tf_op jit(solution)/shard_map/reshape | solution.py:73
  32.2 154.6 %all-reduce.2.cloned.1.call-done = bf16[512,2,1536]{2,0,1:T(8,128)(2,1)} async-done(((bf16[512,2,1536]{2,0,1:T(8,128)(2,1)}), bf16[512,2,1536]{2,0,1:T(8,128)(2,1)}) %all-reduce.2.cloned.1.call-update) | async-done | bytes 3145744 | tf_op jit(solution)/shard_map/psum | solution.py:71
  186.9 1.1 multiply_convert_fusion
  187.9 0.5 convert_element_type.49
  188.4 0.1 copy.39
  188.5 24.4 %all_to_all.15 = bf16[32,2,2,16,96]{4,3,1,2,0:T(8,128)(2,1)S(1)} all-to-all(bf16[32,2,2,16,96]{4,3,1,2,0:T(8,128)(2,1)S(1)} %copy.39), channel_id=1, replica_groups=mesh['tm'=32,'cell'=8] {'tm'}, dimensions={0} | all-to-all | bytes 786432 | tf_op jit(solution)/shard_map/all_to_all | solution.py:80
  213.0 0.4 fusion.25
  213.4 0.4 fusion.26
  213.8 0.4 convolution_add_fusion.1
  214.2 0.4 convolution_subtract_fusion.1
  214.7 5.1 %fusion.12 = f32[2,96,512]{2,1,0:T(8,128)S(1)} fusion(f32[2,512,96]{1,2,0:T(8,128)S(1)} %convolution_subtract_fusion.1), kind=kOutput, calls=%fused_computation.24 | convolution fusion | flops 607649792 | bytes 786432 | tf_op jit(solution)/shard_map/qts,tw->qsw/dot_general | solution.py:32
  219.8 5.1 %fusion.14 = f32[2,96,512]{2,1,0:T(8,128)S(1)} fusion(f32[2,512,96]{1,2,0:T(8,128)S(1)} %convolution_add_fusion.1), kind=kOutput, calls=%fused_computation.26 | convolution fusion | flops 607649792 | bytes 786432 | tf_op jit(solution)/shard_map/qts,tw->qsw/dot_general | solution.py:29
  224.8 5.1 %fusion = f32[2,96,512]{2,1,0:T(8,128)S(1)} fusion(f32[2,96,512]{2,1,0:T(8,128)S(1)} %fusion.12, f32[2,512,96]{1,2,0:T(8,128)S(1)} %convolution_add_fusion.1), kind=kOutput, calls=%fused_computation.8 | convolution fusion | flops 607846400 | bytes 1179648 | tf_op jit(solution)/shard_map/qts,tw->qsw/dot_general | solution.py:32
  229.9 5.6 %fusion.3 = f32[2,96,512]{2,1,0:T(8,128)} fusion(f32[2,96,512]{2,1,0:T(8,128)S(1)} %fusion, f32[2,96,512]{2,1,0:T(8,128)S(1)} %fusion.14, f32[2,512,96]{1,2,0:T(8,128)S(1)} %convolution_subtract_fusion.1), kind=kOutput, calls=%fused_computation.14 | convolution fusion | flops 608043008 | bytes 1572864 | tf_op jit(solution)/shard_map/qts,tw->qsw/dot_general | solution.py:29
  (8 shorter events, 0.1 us)
Async XLA Ops:
  6.5 9.7 %copy-start = (bf16[512,16,96]{0,2,1:T(8,128)(2,1)S(1)}, bf16[512,16,96]{0,2,1:T(8,128)(2,1)}, u32[]{:S(2)}) copy-start(bf16[512,16,96]{0,2,1:T(8,128)(2,1)} %param.4) | copy-start | bytes 4718596
  6.5 180.3 %all-reduce.2.cloned.1.call-start = ((), (), s32[]{:S(2)}) async-start(), calls=%async_computation.1 | async-start | bytes 6291456 | tf_op jit(solution)/shard_map/psum | solution.py:71
  32.2 180.7 %copy-start.1 = (f32[2,2,96,96]{3,2,1,0:T(8,128)S(1)}, f32[2,2,96,96]{3,2,1,0:T(8,128)}, u32[]{:S(2)}) copy-start(f32[2,2,96,96]{3,2,1,0:T(8,128)} %param.7) | copy-start | bytes 442372
Sparse Core Ops, SparseCore 0:
  32.4 154.4 all-reduce.1
where the time goes:
time: 243 us; the launch traced here: 242 us
  waiting for transfers between devices  155 us (64%)
  matrix products  27.3 us (11%)
  blocking collectives  24.4 us (10%)
  local copies, waits for them, and re-layouts  16.4 us (7%)
  between operations  13.5 us (6%)
  other arithmetic  6.14 us (3%)
    psum x1, waiting for transfers between devices, local(): lax.psum(partial_term.astype(jnp.bfloat16), 'cell').astype(jnp.float32)  155 us
    all_to_all x1, blocking collectives, local(): lax.all_to_all(blocks.astype(jnp.bfloat16), 'tm', split_axis=0, concat_ax...  24.4 us
    reshape x2, local copies, waits for them, and re-layouts, local(): summed = lax.psum(partial_term.astype(jnp.bfloat16), 'cell').astype(jnp.f...  11.2 us
    dot_general x1, matrix products, fourier(): jnp.einsum(form, imag_in, sines, precision=largest_value)  5.61 us
    dot_general x1, matrix products, fourier(): jnp.einsum(form, real_in, cosines, precision=largest_value)  5.08 us
    dot_general x1, matrix products, fourier(): jnp.einsum(form, imag_in, cosines, precision=largest_value)  5.08 us
    dot_general x1, matrix products, fourier(): jnp.einsum(form, real_in, sines, precision=largest_value)  5.08 us
    another operation x1, other arithmetic  4.98 us
  transfers between devices with their start and end apart: 1, of which 1 were waited for; matrix products, arithmetic and copies ran while one was open for 0% of the time, Pallas kernels for 0%

commit v1 on v0

--- a/solution.py
+++ b/solution.py
@@ -68,7 +68,7 @@
         preferred_element_type=jnp.float32,
     )
     summed = (
-        lax.psum(partial_term.astype(jnp.bfloat16), "cell")
+        jnp.sum(lax.all_gather(partial_term.astype(jnp.bfloat16), "cell"), 0)
         .astype(jnp.float32)
         .reshape(q_total, 2, frames_dev * branches)
     )

time: 243 us -> 368 us (1.51)
  waiting for transfers between devices: 155 us -> 267 us
  other arithmetic: 6.14 us -> 20.7 us
    all_gather x0 -> x1, waiting for transfers between devices: none -> 267 us  [local(): lax.all_gather(partial_term.astype(jnp.bfloat16), 'cell')]
    psum x1 -> x0, waiting for transfers between devices: 155 us -> none  [local(): lax.psum(partial_term.astype(jnp.bfloat16), 'cell').astype(jnp.float32)]
    reduce_sum x0 -> x1, other arithmetic: none -> 15.5 us  [local(): jnp.sum(lax.all_gather(partial_term.astype(jnp.bfloat16), 'cell'), 0)]
    reshape x2 -> x0, local copies, waits for them, and re-layouts: 11.2 us -> none  [local(): summed = lax.psum(partial_term.astype(jnp.bfloat16), 'cell').astype(jnp.f...]
    convert_element_type x0 -> x1, local copies, waits for them, and re-layouts: none -> 7.76 us  [local(): summed = jnp.sum(lax.all_gather(partial_term.astype(jnp.bfloat16), 'cell'...]
where the time goes in v1:
time: 368 us; the launch traced here: 367 us
  waiting for transfers between devices  267 us (73%)
  matrix products  27.3 us (7%)
  blocking collectives  24.6 us (7%)
  other arithmetic  20.7 us (6%)
  local copies, waits for them, and re-layouts  14.1 us (4%)
  between operations  13.5 us (4%)
    all_gather x1, waiting for transfers between devices, local(): lax.all_gather(partial_term.astype(jnp.bfloat16), 'cell')  267 us
    all_to_all x1, blocking collectives, local(): lax.all_to_all(blocks.astype(jnp.bfloat16), 'tm', split_axis=0, concat_ax...  24.6 us
    reduce_sum x1, other arithmetic, local(): jnp.sum(lax.all_gather(partial_term.astype(jnp.bfloat16), 'cell'), 0)  15.5 us
    convert_element_type x1, local copies, waits for them, and re-layouts, local(): summed = jnp.sum(lax.all_gather(partial_term.astype(jnp.bfloat16), 'cell'...  7.76 us
  transfers between devices with their start and end apart: 1, of which 1 were waited for; matrix products, arithmetic and copies ran while one was open for 0% of the time, Pallas kernels for 0%

profile of v1, /device:TPU:1, one launch (start us, length us, event | category | flops | bytes accessed | tf_op | source)
XLA Modules:
  0.0 367.4 jit_solution(13637478800574204063)
XLA Ops:
  6.5 1.1 reshape.403
  7.7 0.1 copy.36
  7.8 0.3 reshape.404
  8.0 0.8 fusion.53
  8.9 5.0 %cosine_convert_fusion = (bf16[512,1,512]{2,0,1:T(8,128)(2,1)S(1)}, bf16[512,1,512]{2,0,1:T(8,128)(2,1)S(1)}) fusion(s32[512]{0:T(512)S(1)} %bitcast.75, s32[512]{0:T(512)S(1)} %bitcast.72, s32[512]{0:T(512)S(1)} %bitcast.76, s32[512]{0:T(512)S(1)} %bitcast.73, s32[512]{0:T(512)S(1)} %bitcast.74, s32[512]{0:T(512)S(1)} %bitcast.71), kind=kLoop, calls=%fused_computation.31 | loop fusion | flops 5505024 | bytes 1060864 | tf_op jit(solution)/shard_map/convert.2
  13.8 0.1 pad_maximum_fusion
  14.0 1.1 copy.37
  15.0 1.2 convert_element_type.54
  16.3 4.8 %convolution_convert_fusion = bf16[1024,1536]{1,0:T(8,128)(2,1)} fusion(bf16[1024,512]{1,0:T(8,128)(2,1)} %convert_element_type.54, bf16[512,1536]{0,1:T(8,128)(2,1)S(1)} %bitcast.63), kind=kOutput, calls=%fused_computation | convolution fusion | flops 1612185600 | bytes 5767168 | tf_op jit(solution)/shard_map/dot_general | solution.py:65
  21.1 267.0 %all-gather.3.cloned.1.call-done = bf16[8192,1536]{1,0:T(8,128)(2,1)} async-done(((bf16[1024,1536]{1,0:T(8,128)(2,1)}), bf16[8192,1536]{1,0:T(8,128)(2,1)}) %all-gather.3.cloned.1.call-update) | async-done | bytes 25165840 | tf_op jit(solution)/shard_map/all_gather | solution.py:71
  288.1 15.5 %reduce_sum.12 = bf16[1024,1536]{1,0:T(8,128)(2,1)} reduce(bf16[8,1024,1536]{2,1,0:T(8,128)(2,1)} %bitcast.64, bf16[]{:T(256)} %constant.37.clone.1), dimensions={0}, to_apply=%region_0.1 | reduce | flops 11010048 | bytes 28311554 | tf_op jit(solution)/shard_map/reduce_sum | solution.py:71
  303.6 7.8 %reshape.406 = f32[512,2,1536]{2,1,0:T(2,128)} reshape(bf16[1024,1536]{1,0:T(8,128)(2,1)} %reduce_sum.12) | data formatting | bytes 9437184 | tf_op jit(solution)/shard_map/convert_element_type | solution.py:72
  311.4 1.2 constant_dynamic-slice_fusion
  312.6 0.1 fusion.19
  312.8 0.5 convert_element_type.59
  313.3 24.6 %all_to_all.15 = bf16[32,2,2,16,96]{4,3,1,2,0:T(8,128)(2,1)S(1)} all-to-all(bf16[32,2,2,16,96]{4,3,1,2,0:T(8,128)(2,1)S(1)} %copy.39), channel_id=1, replica_groups=mesh['tm'=32,'cell'=8] {'tm'}, dimensions={0} | all-to-all | bytes 786432 | tf_op jit(solution)/shard_map/all_to_all | solution.py:80
  338.0 0.4 fusion.26
  338.4 0.4 fusion.27
  338.8 0.4 convolution_add_fusion.1
  339.2 0.4 convolution_subtract_fusion.1
  339.7 5.1 %fusion.12 = f32[2,96,512]{2,1,0:T(8,128)S(1)} fusion(f32[2,512,96]{1,2,0:T(8,128)S(1)} %convolution_subtract_fusion.1), kind=kOutput, calls=%fused_computation.24 | convolution fusion | flops 607649792 | bytes 786432 | tf_op jit(solution)/shard_map/qts,tw->qsw/dot_general | solution.py:32
  344.8 5.1 %fusion.14 = f32[2,96,512]{2,1,0:T(8,128)S(1)} fusion(f32[2,512,96]{1,2,0:T(8,128)S(1)} %convolution_add_fusion.1), kind=kOutput, calls=%fused_computation.26 | convolution fusion | flops 607649792 | bytes 786432 | tf_op jit(solution)/shard_map/qts,tw->qsw/dot_general | solution.py:29
  349.9 5.1 %fusion = f32[2,96,512]{2,1,0:T(8,128)S(1)} fusion(f32[2,96,512]{2,1,0:T(8,128)S(1)} %fusion.12, f32[2,512,96]{1,2,0:T(8,128)S(1)} %convolution_add_fusion.1), kind=kOutput, calls=%fused_computation.8 | convolution fusion | flops 607846400 | bytes 1179648 | tf_op jit(solution)/shard_map/qts,tw->qsw/dot_general | solution.py:32
  354.9 5.6 %fusion.3 = f32[2,96,512]{2,1,0:T(8,128)} fusion(f32[2,96,512]{2,1,0:T(8,128)S(1)} %fusion, f32[2,96,512]{2,1,0:T(8,128)S(1)} %fusion.14, f32[2,512,96]{1,2,0:T(8,128)S(1)} %convolution_subtract_fusion.1), kind=kOutput, calls=%fused_computation.14 | convolution fusion | flops 608043008 | bytes 1572864 | tf_op jit(solution)/shard_map/qts,tw->qsw/dot_general | solution.py:29
  (9 shorter events, 0.1 us)
Async XLA Ops:
  6.5 9.7 %copy-start = (bf16[512,16,96]{0,2,1:T(8,128)(2,1)S(1)}, bf16[512,16,96]{0,2,1:T(8,128)(2,1)}, u32[]{:S(2)}) copy-start(bf16[512,16,96]{0,2,1:T(8,128)(2,1)} %param.4) | copy-start | bytes 4718596
  6.5 281.6 %all-gather.3.cloned.1.call-start = ((), (), s32[]{:S(2)}) async-start(), calls=%async_computation.1 | async-start | bytes 28311552 | tf_op jit(solution)/shard_map/all_gather | solution.py:71
  311.4 26.6 %copy-start.1 = (f32[2,2,96,96]{3,2,1,0:T(8,128)S(1)}, f32[2,2,96,96]{3,2,1,0:T(8,128)}, u32[]{:S(2)}) copy-start(f32[2,2,96,96]{3,2,1,0:T(8,128)} %param.7) | copy-start | bytes 442372
Sparse Core Ops, SparseCore 0:
  21.2 266.8 all-gather.2
